TPU v7x, 32 devices: a whole 2x2x4 slice. The times are simulated.
32 devices in a mesh: mol: 2 (over x), occ: 16 (over z, y, core).
Axes of the slice: x: 2, y: 2, z: 4, core: 2. Of those that a mesh axis runs over, the one named last changes fastest.
Arguments:
- integrals: bfloat16 [512, 128, 2048], P(('mol', 'occ')), parts along dimension 0, may hold values from -6 to 6
- orbitals: bfloat16 [4096, 1536], P('mol'), parts along dimension 0
- occ_energy: float32 [256], P('mol'), parts along dimension 0, may hold values from -2 to -0.3
- vir_energy: float32 [3072], P('mol'), parts along dimension 0, may hold values from 0.1 to 3
- owner: int32 [16], P('mol'), parts along dimension 0, may hold values from 0 to 127
- vblock: int32 [16], P('mol'), parts along dimension 0, may hold values from 0 to 7
Outputs:
- factors: bfloat16 [512, 128, 1536], P('mol', 'occ'), parts along dimension 0
- pair_energy: float32 [256, 8], P(('mol', 'occ')), parts along dimension 0
There are 2 independent parts, one for each index of `mol`. A program takes and returns all parts, laid end to end along the dimension named above; each array names one. Nothing has to cross between parts.
Inputs may be any that keep to these rules, and one draw needn't show every extreme that they name: `owner`: each step names one occupied orbital and one virtual block; steps may repeat.
All inputs are finite; a program needn't handle non-finite values.
Results may differ from a plain program's by a relative error of at most 0.001.
Values may be sent and summed in bfloat16 or wider, within the bound.
No kernel may reach another device: no remote copies, remote signals or barrier semaphores. Data moves between devices by JAX's collectives and lax.ppermute only.
A program may use at most 128 MiB of HBM per device.

v0:
```python
import jax
import jax.numpy as jnp
from jax import lax
from jax.sharding import PartitionSpec as P

VBLK = 192


def pair_column(factors, block, occ_here, occ_energy, vir_energy, orbital_j, block_id):
    coulomb = lax.dot_general(
        factors, block, (((0,), (0,)), ((), ())), preferred_element_type=jnp.float32
    )
    vir_block = lax.dynamic_slice(vir_energy, (block_id * VBLK,), (VBLK,))
    occ_j = occ_energy[orbital_j]
    denom = vir_energy[None, :, None] + vir_block[None, None, :] - occ_here[:, None, None] - occ_j
    scale = 1.0 / (factors.shape[0] * vir_energy.shape[0] * VBLK)
    return -jnp.sum(coulomb * coulomb / denom, axis=(1, 2)) * scale


def per_device(integrals, orbitals, occ_energy, vir_energy, owner, vblock):
    aux_here, occ_total, basis_count = integrals.shape
    step_count = owner.shape[0]
    flat = integrals.reshape(aux_here * occ_total, basis_count)
    product = jnp.dot(flat, orbitals, preferred_element_type=jnp.float32).astype(jnp.bfloat16)
    product = product.reshape(aux_here, occ_total, orbitals.shape[1])

    def own_piece(step):
        piece = lax.dynamic_slice(
            product, (jnp.int32(0), owner[step], vblock[step] * VBLK), (aux_here, 1, VBLK)
        )
        return piece[:, 0, :]

    pieces = jnp.stack([own_piece(step) for step in range(step_count)], axis=1)
    blocks = lax.all_gather(pieces, "occ", axis=0, tiled=True)
    factors = lax.all_to_all(product, "occ", split_axis=1, concat_axis=0, tiled=True)
    local_count = factors.shape[1]
    occ_here = lax.dynamic_slice(occ_energy, (lax.axis_index("occ") * local_count,), (local_count,))
    energies = jnp.zeros((local_count, step_count), jnp.float32)

    def step_body(step, energies):
        orbital_j = owner[step]
        block_id = vblock[step]
        block = lax.dynamic_index_in_dim(blocks, step, axis=1, keepdims=False)
        column = pair_column(factors, block, occ_here, occ_energy, vir_energy, orbital_j, block_id)
        return lax.dynamic_update_slice(energies, column[:, None], (jnp.int32(0), step))

    energies = lax.fori_loop(0, step_count, step_body, energies)
    return (factors, energies)


def solution(mesh):
    placed = (P(("mol", "occ"), None, None), P("mol", None), P("mol"), P("mol"), P("mol"), P("mol"))
    return jax.shard_map(
        per_device,
        mesh=mesh,
        in_specs=placed,
        out_specs=(P("mol", "occ", None), P(("mol", "occ"), None)),
        check_vma=False,
    )
```

profile of v0, /device:TPU:9, one launch (start us, length us, event | category | flops | bytes accessed | tf_op | source)
XLA Modules:
  0.0 285.7 jit_solution(6650717841820332586)
XLA Ops:
  0.6 17.3 %convolution_convert_fusion = bf16[2048,1536]{1,0:T(8,128)(2,1)S(1)} fusion(bf16[2048,2048]{1,0:T(8,128)(2,1)} %bitcast.56, bf16[2048,1536]{1,0:T(8,128)(2,1)} %param.9), kind=kOutput, calls=%fused_computation.7 | convolution fusion | flops 12888047616 | bytes 20971520 | tf_op jit(solution)/shard_map/dot_general | solution.py:24
  17.9 2.6 copy-done.1
  20.5 6.2 %copy.19 = bf16[16,128,1536]{2,0,1:T(8,128)(2,1)} copy(bf16[16,128,1536]{2,1,0:T(8,128)(2,1)S(1)} %bitcast.54) | data formatting | bytes 12582912 | tf_op jit(solution)/shard_map/reshape | solution.py:25
  26.8 6.7 %all-to-all-start = ((bf16[16,128,1536]{2,0,1:T(8,128)(2,1)}), bf16[16,128,1536]{2,0,1:T(8,128)(2,1)}, u32[]{:S(2)}, u32[]{:S(2)}) async-start(bf16[16,128,1536]{2,0,1:T(8,128)(2,1)} %copy.19), calls=%async_computation | async-start | bytes 12582912 | tf_op jit(solution)/shard_map/all_to_all | solution.py:35
  33.5 0.7 fusion.4
  39.2 0.7 fusion.5
  55.2 1.5 constant_dynamic-slice_fusion
  56.8 0.2 stack.3
  57.0 127.9 %all_gather.3 = bf16[256,8,192]{2,1,0:T(8,128)(2,1)S(1)} all-gather(bf16[16,8,192]{2,1,0:T(8,128)(2,1)S(1)} %stack.3), channel_id=1, replica_groups=mesh['mol'=2,'occ'=16] {'occ'}, dimensions={0}, use_global_device_ids=true | all-gather | bytes 835584 | tf_op jit(solution)/shard_map/all_gather | solution.py:34
  184.8 1.0 copy.21
  185.9 0.1 dynamic_slice.71
  185.9 6.9 %copy.20 = bf16[16,16,8,1536]{3,2,1,0:T(8,128)(2,1)S(1)} copy(bf16[16,16,8,1536]{3,1,2,0:T(8,128)(2,1)} %bitcast.10) | data formatting | bytes 12582912 | tf_op jit(solution)/shard_map/all_to_all | solution.py:35
  192.8 0.0 copy-start.2
  192.9 4.7 %copy.22 = bf16[256,8,1536]{2,0,1:T(8,128)(2,1)} copy(bf16[256,8,1536]{2,1,0:T(8,128)(2,1)S(1)} %bitcast.52) | data formatting | bytes 12582912 | tf_op jit(solution)/shard_map/while | solution.py:47
  197.6 87.4 %while.13 = (s32[]{:T(128)}, f32[8,8]{0,1:T(8,128)S(1)}, bf16[256,8,192]{0,2,1:T(8,128)(2,1)S(1)}, bf16[256,8,1536]{2,0,1:T(8,128)(2,1)}, f32[1536]{0:T(1024)S(1...) while((s32[]{:T(128)}, f32[8,8]{0,1:T(8,128)S(1)}, ...), condition=%wide.region_2.3_spmd, body=%wide.region_0.2_spmd.sunk | while | flops 1220050944 | bytes 8758441 | solution.py:47
  197.6 0.6 dynamic_slice.92
  198.8 0.1 dynamic_slice.93
  198.9 0.1 broadcast_add_fusion.2
  199.1 0.6 dynamic_slice.90
  201.6 0.6 dynamic_slice.91
  202.2 6.3 %fusion.14 = f32[8]{0:T(128)S(1)} fusion(bf16[256,8,1536]{2,0,1:T(8,128)(2,1)} %get-tuple-element.307, f32[]{:T(128)} %bitcast.50, f32[8]{0:T(128)S(1)} %get-tuple-element.310, f32[1536,192]{0,1:T(8,128)S(1)} %broadcast_add_fusion.2, bf16[256,8,192]{0,2,1:T(8,128)(2,1)S(1)} %get-tuple-element.306, s32[]{:T(128)} %get-tuple-element.290), kind=kOutput, calls=%fused_computation.1.clone.1 | convolution fusion | flops 1219756032 | bytes 7569960 | tf_op jit(solution)/shard_map/while/body/eval_jaxpr/dot_general | solution.py:10
  208.5 0.6 dynamic_slice.92
  209.8 0.1 dynamic_slice.93
  209.8 0.1 broadcast_add_fusion.2
  210.0 0.6 dynamic_slice.90
  212.5 0.6 dynamic_slice.91
  213.1 6.3 %fusion.14 = f32[8]{0:T(128)S(1)} fusion(bf16[256,8,1536]{2,0,1:T(8,128)(2,1)} %get-tuple-element.307, f32[]{:T(128)} %bitcast.50, f32[8]{0:T(128)S(1)} %get-tuple-element.310, f32[1536,192]{0,1:T(8,128)S(1)} %broadcast_add_fusion.2, bf16[256,8,192]{0,2,1:T(8,128)(2,1)S(1)} %get-tuple-element.306, s32[]{:T(128)} %get-tuple-element.290), kind=kOutput, calls=%fused_computation.1.clone.1 | convolution fusion | flops 1219756032 | bytes 7569960 | tf_op jit(solution)/shard_map/while/body/eval_jaxpr/dot_general | solution.py:10
  219.4 0.6 dynamic_slice.92
  220.7 0.1 dynamic_slice.93
  220.8 0.1 broadcast_add_fusion.2
  220.9 0.6 dynamic_slice.90
  223.5 0.6 dynamic_slice.91
  224.1 6.3 %fusion.14 = f32[8]{0:T(128)S(1)} fusion(bf16[256,8,1536]{2,0,1:T(8,128)(2,1)} %get-tuple-element.307, f32[]{:T(128)} %bitcast.50, f32[8]{0:T(128)S(1)} %get-tuple-element.310, f32[1536,192]{0,1:T(8,128)S(1)} %broadcast_add_fusion.2, bf16[256,8,192]{0,2,1:T(8,128)(2,1)S(1)} %get-tuple-element.306, s32[]{:T(128)} %get-tuple-element.290), kind=kOutput, calls=%fused_computation.1.clone.1 | convolution fusion | flops 1219756032 | bytes 7569960 | tf_op jit(solution)/shard_map/while/body/eval_jaxpr/dot_general | solution.py:10
  230.4 0.6 dynamic_slice.92
  231.6 0.1 dynamic_slice.93
  231.7 0.1 broadcast_add_fusion.2
  231.9 0.6 dynamic_slice.90
  234.4 0.6 dynamic_slice.91
  235.0 6.3 %fusion.14 = f32[8]{0:T(128)S(1)} fusion(bf16[256,8,1536]{2,0,1:T(8,128)(2,1)} %get-tuple-element.307, f32[]{:T(128)} %bitcast.50, f32[8]{0:T(128)S(1)} %get-tuple-element.310, f32[1536,192]{0,1:T(8,128)S(1)} %broadcast_add_fusion.2, bf16[256,8,192]{0,2,1:T(8,128)(2,1)S(1)} %get-tuple-element.306, s32[]{:T(128)} %get-tuple-element.290), kind=kOutput, calls=%fused_computation.1.clone.1 | convolution fusion | flops 1219756032 | bytes 7569960 | tf_op jit(solution)/shard_map/while/body/eval_jaxpr/dot_general | solution.py:10
  241.3 0.6 dynamic_slice.92
  242.6 0.1 dynamic_slice.93
  242.6 0.1 broadcast_add_fusion.2
  242.8 0.6 dynamic_slice.90
  245.3 0.6 dynamic_slice.91
  245.9 6.3 %fusion.14 = f32[8]{0:T(128)S(1)} fusion(bf16[256,8,1536]{2,0,1:T(8,128)(2,1)} %get-tuple-element.307, f32[]{:T(128)} %bitcast.50, f32[8]{0:T(128)S(1)} %get-tuple-element.310, f32[1536,192]{0,1:T(8,128)S(1)} %broadcast_add_fusion.2, bf16[256,8,192]{0,2,1:T(8,128)(2,1)S(1)} %get-tuple-element.306, s32[]{:T(128)} %get-tuple-element.290), kind=kOutput, calls=%fused_computation.1.clone.1 | convolution fusion | flops 1219756032 | bytes 7569960 | tf_op jit(solution)/shard_map/while/body/eval_jaxpr/dot_general | solution.py:10
  252.2 0.6 dynamic_slice.92
  253.5 0.1 dynamic_slice.93
  253.6 0.1 broadcast_add_fusion.2
  253.7 0.6 dynamic_slice.90
  256.2 0.6 dynamic_slice.91
  256.9 6.3 %fusion.14 = f32[8]{0:T(128)S(1)} fusion(bf16[256,8,1536]{2,0,1:T(8,128)(2,1)} %get-tuple-element.307, f32[]{:T(128)} %bitcast.50, f32[8]{0:T(128)S(1)} %get-tuple-element.310, f32[1536,192]{0,1:T(8,128)S(1)} %broadcast_add_fusion.2, bf16[256,8,192]{0,2,1:T(8,128)(2,1)S(1)} %get-tuple-element.306, s32[]{:T(128)} %get-tuple-element.290), kind=kOutput, calls=%fused_computation.1.clone.1 | convolution fusion | flops 1219756032 | bytes 7569960 | tf_op jit(solution)/shard_map/while/body/eval_jaxpr/dot_general | solution.py:10
  263.2 0.6 dynamic_slice.92
  264.4 0.1 dynamic_slice.93
  264.5 0.1 broadcast_add_fusion.2
  264.7 0.6 dynamic_slice.90
  267.2 0.6 dynamic_slice.91
  267.8 6.3 %fusion.14 = f32[8]{0:T(128)S(1)} fusion(bf16[256,8,1536]{2,0,1:T(8,128)(2,1)} %get-tuple-element.307, f32[]{:T(128)} %bitcast.50, f32[8]{0:T(128)S(1)} %get-tuple-element.310, f32[1536,192]{0,1:T(8,128)S(1)} %broadcast_add_fusion.2, bf16[256,8,192]{0,2,1:T(8,128)(2,1)S(1)} %get-tuple-element.306, s32[]{:T(128)} %get-tuple-element.290), kind=kOutput, calls=%fused_computation.1.clone.1 | convolution fusion | flops 1219756032 | bytes 7569960 | tf_op jit(solution)/shard_map/while/body/eval_jaxpr/dot_general | solution.py:10
  274.1 0.6 dynamic_slice.92
  275.4 0.1 dynamic_slice.93
  275.4 0.1 broadcast_add_fusion.2
  275.6 0.6 dynamic_slice.90
  278.1 0.6 dynamic_slice.91
  278.7 6.3 %fusion.14 = f32[8]{0:T(128)S(1)} fusion(bf16[256,8,1536]{2,0,1:T(8,128)(2,1)} %get-tuple-element.307, f32[]{:T(128)} %bitcast.50, f32[8]{0:T(128)S(1)} %get-tuple-element.310, f32[1536,192]{0,1:T(8,128)S(1)} %broadcast_add_fusion.2, bf16[256,8,192]{0,2,1:T(8,128)(2,1)S(1)} %get-tuple-element.306, s32[]{:T(128)} %get-tuple-element.290), kind=kOutput, calls=%fused_computation.1.clone.1 | convolution fusion | flops 1219756032 | bytes 7569960 | tf_op jit(solution)/shard_map/while/body/eval_jaxpr/dot_general | solution.py:10
  285.0 0.7 copy.23
  (28 shorter events, 0.3 us)
Async XLA Ops:
  17.9 2.6 copy-start.1
  26.7 6.8 %copy-start.4 = (s32[8]{0:T(128)S(1)}, s32[8]{0:T(128)}, u32[]{:S(2)}) copy-start(s32[8]{0:T(128)} %param.13) | copy-start | bytes 100
  26.7 12.5 %copy-start.3 = (s32[8]{0:T(128)S(1)}, s32[8]{0:T(128)}, u32[]{:S(2)}) copy-start(s32[8]{0:T(128)} %param.12) | copy-start | bytes 100
  26.7 159.1 %copy-start.5 = (f32[128]{0:T(128)S(1)}, f32[128]{0:T(128)}, u32[]{:S(2)}) copy-start(f32[128]{0:T(128)} %param.10) | copy-start | bytes 1540
  26.8 159.2 %all-to-all-start = ((bf16[16,128,1536]{2,0,1:T(8,128)(2,1)}), bf16[16,128,1536]{2,0,1:T(8,128)(2,1)}, u32[]{:S(2)}, u32[]{:S(2)}) async-start(bf16[16,128,1536]{2,0,1:T(8,128)(2,1)} %copy.19), calls=%async_computation | async-start | bytes 12582912 | tf_op jit(solution)/shard_map/all_to_all | solution.py:35
  192.8 4.7 %copy-start = (bf16[16,16,8,1536]{3,2,1,0:T(8,128)(2,1)}, bf16[16,16,8,1536]{3,2,1,0:T(8,128)(2,1)S(1)}, u32[]{:S(2)}) copy-start(bf16[16,16,8,1536]{3,2,1,0:T(8,128)(2,1)S(1)} %copy.20) | copy-start | bytes 18874372
  192.8 4.7 %copy-start.2 = (f32[1536]{0:T(1024)S(1)}, f32[1536]{0:T(1024)}, u32[]{:S(2)}) copy-start(f32[1536]{0:T(1024)} %param.11) | copy-start | bytes 18436
where the time goes:
time: 287 us; the launch traced here: 286 us
  blocking collectives  128 us (45%)
  matrix products  67.4 us (23%)
  local copies, waits for them, and re-layouts  40.8 us (14%)
  between operations  21.1 us (7%)
  loops' own time  20.6 us (7%)
  starting transfers between devices  6.74 us (2%)
    all_gather x1, blocking collectives, per_device(): blocks = lax.all_gather(pieces, 'occ', axis=0, tiled=True)  128 us
    dot_general x8, matrix products, pair_column(): lax.dot_general(factors, block, (((0,), (0,)), ((), ())), preferred_eleme...  50.1 us
    another operation x1, loops' own time, per_device(): energies = lax.fori_loop(0, step_count, step_body, energies)  20.6 us
    dot_general x1, matrix products, per_device(): jnp.dot(flat, orbitals, preferred_element_type=jnp.float32)  17.3 us
    all_to_all x1, local copies, waits for them, and re-layouts, per_device(): lax.all_to_all(product, 'occ', split_axis=1, concat_axis=0, tiled=True)  6.9 us
    all_to_all x1, starting transfers between devices, per_device(): lax.all_to_all(product, 'occ', split_axis=1, concat_axis=0, tiled=True)  6.74 us
    reshape x1, local copies, waits for them, and re-layouts, per_device(): product = product.reshape(aux_here, occ_total, orbitals.shape[1])  6.2 us
  transfers between devices with their start and end apart: 1, of which 0 were waited for; matrix products, arithmetic and copies ran while one was open for 1% of the time, Pallas kernels for 0%

commit v1 on v0

--- a/solution.py
+++ b/solution.py
@@ -31,7 +31,16 @@
         return piece[:, 0, :]
 
     pieces = jnp.stack([own_piece(step) for step in range(step_count)], axis=1)
-    blocks = lax.all_gather(pieces, "occ", axis=0, tiled=True)
+    ways = lax.axis_size("occ")
+    up = [(d, (d + 1) % ways) for d in range(ways)]
+    down = [(d, (d - 1) % ways) for d in range(ways)]
+    earlier, later = ([pieces], [pieces])
+    for _ in range(ways // 2):
+        earlier.append(lax.ppermute(earlier[-1], "occ", up))
+    for _ in range((ways - 1) // 2):
+        later.append(lax.ppermute(later[-1], "occ", down))
+    line = jnp.concatenate([*earlier[::-1], *later[1:]], axis=0)
+    blocks = jnp.roll(line, (lax.axis_index("occ") - ways // 2) * pieces.shape[0], axis=0)
     factors = lax.all_to_all(product, "occ", split_axis=1, concat_axis=0, tiled=True)
     local_count = factors.shape[1]
     occ_here = lax.dynamic_slice(occ_energy, (lax.axis_index("occ") * local_count,), (local_count,))

time: 287 us -> 308 us (1.073); the launches traced: 286 us -> 302 us
  starting transfers between devices: 6.74 us -> 136 us
  blocking collectives: 128 us -> 0 us
  waiting for transfers between devices: 0.01 us -> 15 us
    ppermute x0 -> x15, starting transfers between devices: none -> 129 us  [the longest x7 76.9 us: per_device(): later.append(lax.ppermute(later[-1], 'occ', down))]
    all_gather x1 -> x0, blocking collectives: 128 us -> none  [per_device(): blocks = lax.all_gather(pieces, 'occ', axis=0, tiled=True)]
    ppermute x0 -> x15, waiting for transfers between devices: none -> 15 us  [the longest x7 10.6 us: per_device(): later.append(lax.ppermute(later[-1], 'occ', down))]
  transfers between devices with their start and end apart: 1 -> 16, of which waited for: 0 -> 15; matrix products, arithmetic and copies ran while one was open for 1% -> 1% of each run, Pallas kernels for 0% -> 0%
where the time goes in v1:
time: 308 us; the launch traced here: 302 us
  starting transfers between devices  136 us (44%)
  matrix products  67.4 us (22%)
  local copies, waits for them, and re-layouts  41 us (13%)
  between operations  21 us (7%)
  loops' own time  20.6 us (7%)
  waiting for transfers between devices  15 us (5%)
    ppermute x7, starting transfers between devices, per_device(): later.append(lax.ppermute(later[-1], 'occ', down))  76.9 us
    ppermute x8, starting transfers between devices, per_device(): earlier.append(lax.ppermute(earlier[-1], 'occ', up))  52.4 us
    dot_general x8, matrix products, pair_column(): lax.dot_general(factors, block, (((0,), (0,)), ((), ())), preferred_eleme...  50.1 us
    another operation x1, loops' own time, per_device(): energies = lax.fori_loop(0, step_count, step_body, energies)  20.6 us
    dot_general x1, matrix products, per_device(): jnp.dot(flat, orbitals, preferred_element_type=jnp.float32)  17.3 us
    ppermute x7, waiting for transfers between devices, per_device(): later.append(lax.ppermute(later[-1], 'occ', down))  10.6 us
    all_to_all x1, local copies, waits for them, and re-layouts, per_device(): lax.all_to_all(product, 'occ', split_axis=1, concat_axis=0, tiled=True)  6.9 us
    all_to_all x1, starting transfers between devices, per_device(): lax.all_to_all(product, 'occ', split_axis=1, concat_axis=0, tiled=True)  6.74 us
  transfers between devices with their start and end apart: 16, of which 15 were waited for; matrix products, arithmetic and copies ran while one was open for 1% of the time, Pallas kernels for 0%

profile of v1, /device:TPU:9, one launch (start us, length us, event | category | flops | bytes accessed | tf_op | source)
XLA Modules:
  0.0 302.3 jit_solution(3350813820761481469)
XLA Ops:
  0.6 17.3 %convolution_convert_fusion = bf16[2048,1536]{1,0:T(8,128)(2,1)S(1)} fusion(bf16[2048,2048]{1,0:T(8,128)(2,1)} %bitcast.56, bf16[2048,1536]{1,0:T(8,128)(2,1)} %param.9), kind=kOutput, calls=%fused_computation.7 | convolution fusion | flops 12888047616 | bytes 20971520 | tf_op jit(solution)/shard_map/dot_general | solution.py:24
  17.9 2.6 copy-done.1
  20.5 6.2 %copy.19 = bf16[16,128,1536]{2,0,1:T(8,128)(2,1)} copy(bf16[16,128,1536]{2,1,0:T(8,128)(2,1)S(1)} %bitcast.54) | data formatting | bytes 12582912 | tf_op jit(solution)/shard_map/reshape | solution.py:25
  26.7 6.7 %all-to-all-start = ((bf16[16,128,1536]{2,0,1:T(8,128)(2,1)}), bf16[16,128,1536]{2,0,1:T(8,128)(2,1)}, u32[]{:S(2)}, u32[]{:S(2)}) async-start(bf16[16,128,1536]{2,0,1:T(8,128)(2,1)} %copy.19), calls=%async_computation | async-start | bytes 12582912 | tf_op jit(solution)/shard_map/all_to_all | solution.py:44
  33.5 0.7 fusion.4
  39.0 0.7 fusion.5
  54.9 1.5 constant_dynamic-slice_fusion.1
  56.6 1.5 collective-permute-start
  58.1 2.0 collective-permute-done
  60.2 2.5 collective-permute-start.1
  62.6 76.9 %collective-permute-start.8 = (bf16[16,8,192]{2,1,0:T(8,128)(2,1)S(1)}, bf16[16,8,192]{2,1,0:T(8,128)(2,1)S(1)}, u32[]{:S(2)}, u32[]{:S(2)}) collective-permute-start(bf16[16,8,192]{2,1,0:T(8,128)(2,1)S(1)} %stack.3), channel_id=1, source_target_pairs={{0,15},{1,0},{2,1},{3,2},{4,3},{5,4},{6,5},{7,6},{8,7},{9,8},{10,9... | collective-permute-start | bytes 147464 | tf_op jit(solution)/shard_map/ppermute | solution.py:41
  139.5 0.7 collective-permute-done.1
  140.2 32.0 %collective-permute-start.2 = (bf16[16,8,192]{2,1,0:T(8,128)(2,1)S(1)}, bf16[16,8,192]{2,1,0:T(8,128)(2,1)S(1)}, u32[]{:S(2)}, u32[]{:S(2)}) collective-permute-start(bf16[16,8,192]{2,1,0:T(8,128)(2,1)S(1)} %collective-permute-done.1), channel_id=1, source_target_pairs={{0,1},{1,2},{2,3},{3,4},{4,5},{5,6},{6,7},{7,8},{8,9},{9,10},{10,1... | collective-permute-start | bytes 147464 | tf_op jit(solution)/shard_map/ppermute | solution.py:39
  172.2 1.0 collective-permute-done.8
  173.3 0.3 collective-permute-done.2
  173.6 3.4 %collective-permute-start.3 = (bf16[16,8,192]{2,1,0:T(8,128)(2,1)S(1)}, bf16[16,8,192]{2,1,0:T(8,128)(2,1)S(1)}, u32[]{:S(2)}, u32[]{:S(2)}) collective-permute-start(bf16[16,8,192]{2,1,0:T(8,128)(2,1)S(1)} %collective-permute-done.2), channel_id=1, source_target_pairs={{0,1},{1,2},{2,3},{3,4},{4,5},{5,6},{6,7},{7,8},{8,9},{9,10},{10,1... | collective-permute-start | bytes 147464 | tf_op jit(solution)/shard_map/ppermute | solution.py:39
  176.9 1.0 collective-permute-done.9
  178.0 0.3 collective-permute-done.3
  178.3 3.3 %collective-permute-start.4 = (bf16[16,8,192]{2,1,0:T(8,128)(2,1)S(1)}, bf16[16,8,192]{2,1,0:T(8,128)(2,1)S(1)}, u32[]{:S(2)}, u32[]{:S(2)}) collective-permute-start(bf16[16,8,192]{2,1,0:T(8,128)(2,1)S(1)} %collective-permute-done.3), channel_id=1, source_target_pairs={{0,1},{1,2},{2,3},{3,4},{4,5},{5,6},{6,7},{7,8},{8,9},{9,10},{10,1... | collective-permute-start | bytes 147464 | tf_op jit(solution)/shard_map/ppermute | solution.py:39
  181.5 1.0 collective-permute-done.10
  182.9 3.3 %collective-permute-start.5 = (bf16[16,8,192]{2,1,0:T(8,128)(2,1)S(1)}, bf16[16,8,192]{2,1,0:T(8,128)(2,1)S(1)}, u32[]{:S(2)}, u32[]{:S(2)}) collective-permute-start(bf16[16,8,192]{2,1,0:T(8,128)(2,1)S(1)} %collective-permute-done.4), channel_id=1, source_target_pairs={{0,1},{1,2},{2,3},{3,4},{4,5},{5,6},{6,7},{7,8},{8,9},{9,10},{10,1... | collective-permute-start | bytes 147464 | tf_op jit(solution)/shard_map/ppermute | solution.py:39
  186.1 1.0 collective-permute-done.11
  187.5 3.3 %collective-permute-start.6 = (bf16[16,8,192]{2,1,0:T(8,128)(2,1)S(1)}, bf16[16,8,192]{2,1,0:T(8,128)(2,1)S(1)}, u32[]{:S(2)}, u32[]{:S(2)}) collective-permute-start(bf16[16,8,192]{2,1,0:T(8,128)(2,1)S(1)} %collective-permute-done.5), channel_id=1, source_target_pairs={{0,1},{1,2},{2,3},{3,4},{4,5},{5,6},{6,7},{7,8},{8,9},{9,10},{10,1... | collective-permute-start | bytes 147464 | tf_op jit(solution)/shard_map/ppermute | solution.py:39
  190.7 1.0 collective-permute-done.12
  192.0 3.3 %collective-permute-start.7 = (bf16[16,8,192]{2,1,0:T(8,128)(2,1)S(1)}, bf16[16,8,192]{2,1,0:T(8,128)(2,1)S(1)}, u32[]{:S(2)}, u32[]{:S(2)}) collective-permute-start(bf16[16,8,192]{2,1,0:T(8,128)(2,1)S(1)} %collective-permute-done.6), channel_id=1, source_target_pairs={{0,1},{1,2},{2,3},{3,4},{4,5},{5,6},{6,7},{7,8},{8,9},{9,10},{10,1... | collective-permute-start | bytes 147464 | tf_op jit(solution)/shard_map/ppermute | solution.py:39
  195.4 1.0 collective-permute-done.13
  196.8 4.4 %collective-permute-done.14 = bf16[16,8,192]{2,1,0:T(8,128)(2,1)S(1)} collective-permute-done((bf16[16,8,192]{2,1,0:T(8,128)(2,1)S(1)}, bf16[16,8,192]{2,1,0:T(8,128)(2,1)S(1)}, u32[]{:S(2)}, u32[]{:S(2)}) %collective-permute-start.14) | collective-permute-done | bytes 49184 | tf_op jit(solution)/shard_map/ppermute | solution.py:41
  201.5 1.0 copy.21
  202.5 6.9 %copy.20 = bf16[16,16,8,1536]{3,2,1,0:T(8,128)(2,1)S(1)} copy(bf16[16,16,8,1536]{3,1,2,0:T(8,128)(2,1)} %bitcast.10) | data formatting | bytes 12582912 | tf_op jit(solution)/shard_map/all_to_all | solution.py:44
  209.5 4.7 %copy.22 = bf16[256,8,1536]{2,0,1:T(8,128)(2,1)} copy(bf16[256,8,1536]{2,1,0:T(8,128)(2,1)S(1)} %bitcast.52) | data formatting | bytes 12582912 | tf_op jit(solution)/shard_map/while | solution.py:56
  214.2 87.4 %while.13 = (s32[]{:T(128)}, f32[8,8]{0,1:T(8,128)S(1)}, bf16[256,8,192]{0,2,1:T(8,128)(2,1)S(1)}, bf16[256,8,1536]{2,0,1:T(8,128)(2,1)}, f32[1536]{0:T(1024)S(1...) while((s32[]{:T(128)}, f32[8,8]{0,1:T(8,128)S(1)}, ...), condition=%wide.region_2.3_spmd, body=%wide.region_0.2_spmd.sunk | while | flops 1220050944 | bytes 8758441 | solution.py:56
  214.2 0.6 dynamic_slice.98
  215.7 0.6 dynamic_slice.96
  218.2 0.6 dynamic_slice.97
  218.8 6.3 %fusion.14 = f32[8]{0:T(128)S(1)} fusion(bf16[256,8,1536]{2,0,1:T(8,128)(2,1)} %get-tuple-element.307, f32[]{:T(128)} %bitcast.50, f32[8]{0:T(128)S(1)} %get-tuple-element.310, f32[1536,192]{0,1:T(8,128)S(1)} %broadcast_add_fusion.2, bf16[256,8,192]{0,2,1:T(8,128)(2,1)S(1)} %get-tuple-element.306, s32[]{:T(128)} %get-tuple-element.290), kind=kOutput, calls=%fused_computation.1.clone.1 | convolution fusion | flops 1219756032 | bytes 7569960 | tf_op jit(solution)/shard_map/while/body/eval_jaxpr/dot_general | solution.py:10
  225.1 0.6 dynamic_slice.98
  226.6 0.6 dynamic_slice.96
  229.1 0.6 dynamic_slice.97
  229.7 6.3 %fusion.14 = f32[8]{0:T(128)S(1)} fusion(bf16[256,8,1536]{2,0,1:T(8,128)(2,1)} %get-tuple-element.307, f32[]{:T(128)} %bitcast.50, f32[8]{0:T(128)S(1)} %get-tuple-element.310, f32[1536,192]{0,1:T(8,128)S(1)} %broadcast_add_fusion.2, bf16[256,8,192]{0,2,1:T(8,128)(2,1)S(1)} %get-tuple-element.306, s32[]{:T(128)} %get-tuple-element.290), kind=kOutput, calls=%fused_computation.1.clone.1 | convolution fusion | flops 1219756032 | bytes 7569960 | tf_op jit(solution)/shard_map/while/body/eval_jaxpr/dot_general | solution.py:10
  236.0 0.6 dynamic_slice.98
  237.5 0.6 dynamic_slice.96
  240.1 0.6 dynamic_slice.97
  240.7 6.3 %fusion.14 = f32[8]{0:T(128)S(1)} fusion(bf16[256,8,1536]{2,0,1:T(8,128)(2,1)} %get-tuple-element.307, f32[]{:T(128)} %bitcast.50, f32[8]{0:T(128)S(1)} %get-tuple-element.310, f32[1536,192]{0,1:T(8,128)S(1)} %broadcast_add_fusion.2, bf16[256,8,192]{0,2,1:T(8,128)(2,1)S(1)} %get-tuple-element.306, s32[]{:T(128)} %get-tuple-element.290), kind=kOutput, calls=%fused_computation.1.clone.1 | convolution fusion | flops 1219756032 | bytes 7569960 | tf_op jit(solution)/shard_map/while/body/eval_jaxpr/dot_general | solution.py:10
  247.0 0.6 dynamic_slice.98
  248.5 0.6 dynamic_slice.96
  251.0 0.6 dynamic_slice.97
  251.6 6.3 %fusion.14 = f32[8]{0:T(128)S(1)} fusion(bf16[256,8,1536]{2,0,1:T(8,128)(2,1)} %get-tuple-element.307, f32[]{:T(128)} %bitcast.50, f32[8]{0:T(128)S(1)} %get-tuple-element.310, f32[1536,192]{0,1:T(8,128)S(1)} %broadcast_add_fusion.2, bf16[256,8,192]{0,2,1:T(8,128)(2,1)S(1)} %get-tuple-element.306, s32[]{:T(128)} %get-tuple-element.290), kind=kOutput, calls=%fused_computation.1.clone.1 | convolution fusion | flops 1219756032 | bytes 7569960 | tf_op jit(solution)/shard_map/while/body/eval_jaxpr/dot_general | solution.py:10
  257.9 0.6 dynamic_slice.98
  259.4 0.6 dynamic_slice.96
  261.9 0.6 dynamic_slice.97
  262.5 6.3 %fusion.14 = f32[8]{0:T(128)S(1)} fusion(bf16[256,8,1536]{2,0,1:T(8,128)(2,1)} %get-tuple-element.307, f32[]{:T(128)} %bitcast.50, f32[8]{0:T(128)S(1)} %get-tuple-element.310, f32[1536,192]{0,1:T(8,128)S(1)} %broadcast_add_fusion.2, bf16[256,8,192]{0,2,1:T(8,128)(2,1)S(1)} %get-tuple-element.306, s32[]{:T(128)} %get-tuple-element.290), kind=kOutput, calls=%fused_computation.1.clone.1 | convolution fusion | flops 1219756032 | bytes 7569960 | tf_op jit(solution)/shard_map/while/body/eval_jaxpr/dot_general | solution.py:10
  268.8 0.6 dynamic_slice.98
  270.3 0.6 dynamic_slice.96
  272.9 0.6 dynamic_slice.97
  273.5 6.3 %fusion.14 = f32[8]{0:T(128)S(1)} fusion(bf16[256,8,1536]{2,0,1:T(8,128)(2,1)} %get-tuple-element.307, f32[]{:T(128)} %bitcast.50, f32[8]{0:T(128)S(1)} %get-tuple-element.310, f32[1536,192]{0,1:T(8,128)S(1)} %broadcast_add_fusion.2, bf16[256,8,192]{0,2,1:T(8,128)(2,1)S(1)} %get-tuple-element.306, s32[]{:T(128)} %get-tuple-element.290), kind=kOutput, calls=%fused_computation.1.clone.1 | convolution fusion | flops 1219756032 | bytes 7569960 | tf_op jit(solution)/shard_map/while/body/eval_jaxpr/dot_general | solution.py:10
  279.8 0.6 dynamic_slice.98
  281.3 0.6 dynamic_slice.96
  283.8 0.6 dynamic_slice.97
  284.4 6.3 %fusion.14 = f32[8]{0:T(128)S(1)} fusion(bf16[256,8,1536]{2,0,1:T(8,128)(2,1)} %get-tuple-element.307, f32[]{:T(128)} %bitcast.50, f32[8]{0:T(128)S(1)} %get-tuple-element.310, f32[1536,192]{0,1:T(8,128)S(1)} %broadcast_add_fusion.2, bf16[256,8,192]{0,2,1:T(8,128)(2,1)S(1)} %get-tuple-element.306, s32[]{:T(128)} %get-tuple-element.290), kind=kOutput, calls=%fused_computation.1.clone.1 | convolution fusion | flops 1219756032 | bytes 7569960 | tf_op jit(solution)/shard_map/while/body/eval_jaxpr/dot_general | solution.py:10
  290.7 0.6 dynamic_slice.98
  292.2 0.6 dynamic_slice.96
  294.7 0.6 dynamic_slice.97
  295.3 6.3 %fusion.14 = f32[8]{0:T(128)S(1)} fusion(bf16[256,8,1536]{2,0,1:T(8,128)(2,1)} %get-tuple-element.307, f32[]{:T(128)} %bitcast.50, f32[8]{0:T(128)S(1)} %get-tuple-element.310, f32[1536,192]{0,1:T(8,128)S(1)} %broadcast_add_fusion.2, bf16[256,8,192]{0,2,1:T(8,128)(2,1)S(1)} %get-tuple-element.306, s32[]{:T(128)} %get-tuple-element.290), kind=kOutput, calls=%fused_computation.1.clone.1 | convolution fusion | flops 1219756032 | bytes 7569960 | tf_op jit(solution)/shard_map/while/body/eval_jaxpr/dot_general | solution.py:10
  301.6 0.7 copy.23
  (90 shorter events, 3.8 us)
Async XLA Ops:
  17.9 2.6 copy-start.1
  26.7 6.8 %copy-start.4 = (s32[8]{0:T(128)S(1)}, s32[8]{0:T(128)}, u32[]{:S(2)}) copy-start(s32[8]{0:T(128)} %param.13) | copy-start | bytes 100
  26.7 12.3 %copy-start.3 = (s32[8]{0:T(128)S(1)}, s32[8]{0:T(128)}, u32[]{:S(2)}) copy-start(s32[8]{0:T(128)} %param.12) | copy-start | bytes 100
  26.7 168.6 %copy-start.5 = (f32[128]{0:T(128)S(1)}, f32[128]{0:T(128)}, u32[]{:S(2)}) copy-start(f32[128]{0:T(128)} %param.10) | copy-start | bytes 1540
  26.7 175.8 %all-to-all-start = ((bf16[16,128,1536]{2,0,1:T(8,128)(2,1)}), bf16[16,128,1536]{2,0,1:T(8,128)(2,1)}, u32[]{:S(2)}, u32[]{:S(2)}) async-start(bf16[16,128,1536]{2,0,1:T(8,128)(2,1)} %copy.19), calls=%async_computation | async-start | bytes 12582912 | tf_op jit(solution)/shard_map/all_to_all | solution.py:44
  56.6 3.5 %collective-permute-start = (bf16[16,8,192]{2,1,0:T(8,128)(2,1)S(1)}, bf16[16,8,192]{2,1,0:T(8,128)(2,1)S(1)}, u32[]{:S(2)}, u32[]{:S(2)}) collective-permute-start(bf16[16,8,192]{2,1,0:T(8,128)(2,1)S(1)} %stack.3), channel_id=1, source_target_pairs={{0,1},{1,2},{2,3},{3,4},{4,5},{5,6},{6,7},{7,8},{8,9},{9,10},{10,1... | collective-permute-start | bytes 147464 | tf_op jit(solution)/shard_map/ppermute | solution.py:39
  60.2 80.1 %collective-permute-start.1 = (bf16[16,8,192]{2,1,0:T(8,128)(2,1)S(1)}, bf16[16,8,192]{2,1,0:T(8,128)(2,1)S(1)}, u32[]{:S(2)}, u32[]{:S(2)}) collective-permute-start(bf16[16,8,192]{2,1,0:T(8,128)(2,1)S(1)} %collective-permute-done), channel_id=1, source_target_pairs={{0,1},{1,2},{2,3},{3,4},{4,5},{5,6},{6,7},{7,8},{8,9},{9,10},{10,1... | collective-permute-start | bytes 147464 | tf_op jit(solution)/shard_map/ppermute | solution.py:39
  62.6 110.6 %collective-permute-start.8 = (bf16[16,8,192]{2,1,0:T(8,128)(2,1)S(1)}, bf16[16,8,192]{2,1,0:T(8,128)(2,1)S(1)}, u32[]{:S(2)}, u32[]{:S(2)}) collective-permute-start(bf16[16,8,192]{2,1,0:T(8,128)(2,1)S(1)} %stack.3), channel_id=1, source_target_pairs={{0,15},{1,0},{2,1},{3,2},{4,3},{5,4},{6,5},{7,6},{8,7},{9,8},{10,9... | collective-permute-start | bytes 147464 | tf_op jit(solution)/shard_map/ppermute | solution.py:41
  140.2 33.3 %collective-permute-start.2 = (bf16[16,8,192]{2,1,0:T(8,128)(2,1)S(1)}, bf16[16,8,192]{2,1,0:T(8,128)(2,1)S(1)}, u32[]{:S(2)}, u32[]{:S(2)}) collective-permute-start(bf16[16,8,192]{2,1,0:T(8,128)(2,1)S(1)} %collective-permute-done.1), channel_id=1, source_target_pairs={{0,1},{1,2},{2,3},{3,4},{4,5},{5,6},{6,7},{7,8},{8,9},{9,10},{10,1... | collective-permute-start | bytes 147464 | tf_op jit(solution)/shard_map/ppermute | solution.py:39
  173.3 4.7 %collective-permute-start.9 = (bf16[16,8,192]{2,1,0:T(8,128)(2,1)S(1)}, bf16[16,8,192]{2,1,0:T(8,128)(2,1)S(1)}, u32[]{:S(2)}, u32[]{:S(2)}) collective-permute-start(bf16[16,8,192]{2,1,0:T(8,128)(2,1)S(1)} %collective-permute-done.8), channel_id=1, source_target_pairs={{0,15},{1,0},{2,1},{3,2},{4,3},{5,4},{6,5},{7,6},{8,7},{9,8},{10,9... | collective-permute-start | bytes 147464 | tf_op jit(solution)/shard_map/ppermute | solution.py:41
  173.6 4.7 %collective-permute-start.3 = (bf16[16,8,192]{2,1,0:T(8,128)(2,1)S(1)}, bf16[16,8,192]{2,1,0:T(8,128)(2,1)S(1)}, u32[]{:S(2)}, u32[]{:S(2)}) collective-permute-start(bf16[16,8,192]{2,1,0:T(8,128)(2,1)S(1)} %collective-permute-done.2), channel_id=1, source_target_pairs={{0,1},{1,2},{2,3},{3,4},{4,5},{5,6},{6,7},{7,8},{8,9},{9,10},{10,1... | collective-permute-start | bytes 147464 | tf_op jit(solution)/shard_map/ppermute | solution.py:39
  178.0 4.6 %collective-permute-start.10 = (bf16[16,8,192]{2,1,0:T(8,128)(2,1)S(1)}, bf16[16,8,192]{2,1,0:T(8,128)(2,1)S(1)}, u32[]{:S(2)}, u32[]{:S(2)}) collective-permute-start(bf16[16,8,192]{2,1,0:T(8,128)(2,1)S(1)} %collective-permute-done.9), channel_id=1, source_target_pairs={{0,15},{1,0},{2,1},{3,2},{4,3},{5,4},{6,5},{7,6},{8,7},{9,8},{10,9... | collective-permute-start | bytes 147464 | tf_op jit(solution)/shard_map/ppermute | solution.py:41
  178.3 4.6 %collective-permute-start.4 = (bf16[16,8,192]{2,1,0:T(8,128)(2,1)S(1)}, bf16[16,8,192]{2,1,0:T(8,128)(2,1)S(1)}, u32[]{:S(2)}, u32[]{:S(2)}) collective-permute-start(bf16[16,8,192]{2,1,0:T(8,128)(2,1)S(1)} %collective-permute-done.3), channel_id=1, source_target_pairs={{0,1},{1,2},{2,3},{3,4},{4,5},{5,6},{6,7},{7,8},{8,9},{9,10},{10,1... | collective-permute-start | bytes 147464 | tf_op jit(solution)/shard_map/ppermute | solution.py:39
  182.6 4.6 %collective-permute-start.11 = (bf16[16,8,192]{2,1,0:T(8,128)(2,1)S(1)}, bf16[16,8,192]{2,1,0:T(8,128)(2,1)S(1)}, u32[]{:S(2)}, u32[]{:S(2)}) collective-permute-start(bf16[16,8,192]{2,1,0:T(8,128)(2,1)S(1)} %collective-permute-done.10), channel_id=1, source_target_pairs={{0,15},{1,0},{2,1},{3,2},{4,3},{5,4},{6,5},{7,6},{8,7},{9,8},{10,9... | collective-permute-start | bytes 147464 | tf_op jit(solution)/shard_map/ppermute | solution.py:41
  182.9 4.6 %collective-permute-start.5 = (bf16[16,8,192]{2,1,0:T(8,128)(2,1)S(1)}, bf16[16,8,192]{2,1,0:T(8,128)(2,1)S(1)}, u32[]{:S(2)}, u32[]{:S(2)}) collective-permute-start(bf16[16,8,192]{2,1,0:T(8,128)(2,1)S(1)} %collective-permute-done.4), channel_id=1, source_target_pairs={{0,1},{1,2},{2,3},{3,4},{4,5},{5,6},{6,7},{7,8},{8,9},{9,10},{10,1... | collective-permute-start | bytes 147464 | tf_op jit(solution)/shard_map/ppermute | solution.py:39
  187.2 4.6 %collective-permute-start.12 = (bf16[16,8,192]{2,1,0:T(8,128)(2,1)S(1)}, bf16[16,8,192]{2,1,0:T(8,128)(2,1)S(1)}, u32[]{:S(2)}, u32[]{:S(2)}) collective-permute-start(bf16[16,8,192]{2,1,0:T(8,128)(2,1)S(1)} %collective-permute-done.11), channel_id=1, source_target_pairs={{0,15},{1,0},{2,1},{3,2},{4,3},{5,4},{6,5},{7,6},{8,7},{9,8},{10,9... | collective-permute-start | bytes 147464 | tf_op jit(solution)/shard_map/ppermute | solution.py:41
  187.5 4.6 %collective-permute-start.6 = (bf16[16,8,192]{2,1,0:T(8,128)(2,1)S(1)}, bf16[16,8,192]{2,1,0:T(8,128)(2,1)S(1)}, u32[]{:S(2)}, u32[]{:S(2)}) collective-permute-start(bf16[16,8,192]{2,1,0:T(8,128)(2,1)S(1)} %collective-permute-done.5), channel_id=1, source_target_pairs={{0,1},{1,2},{2,3},{3,4},{4,5},{5,6},{6,7},{7,8},{8,9},{9,10},{10,1... | collective-permute-start | bytes 147464 | tf_op jit(solution)/shard_map/ppermute | solution.py:39
  191.8 4.6 %collective-permute-start.13 = (bf16[16,8,192]{2,1,0:T(8,128)(2,1)S(1)}, bf16[16,8,192]{2,1,0:T(8,128)(2,1)S(1)}, u32[]{:S(2)}, u32[]{:S(2)}) collective-permute-start(bf16[16,8,192]{2,1,0:T(8,128)(2,1)S(1)} %collective-permute-done.12), channel_id=1, source_target_pairs={{0,15},{1,0},{2,1},{3,2},{4,3},{5,4},{6,5},{7,6},{8,7},{9,8},{10,9... | collective-permute-start | bytes 147464 | tf_op jit(solution)/shard_map/ppermute | solution.py:41
  192.0 4.6 %collective-permute-start.7 = (bf16[16,8,192]{2,1,0:T(8,128)(2,1)S(1)}, bf16[16,8,192]{2,1,0:T(8,128)(2,1)S(1)}, u32[]{:S(2)}, u32[]{:S(2)}) collective-permute-start(bf16[16,8,192]{2,1,0:T(8,128)(2,1)S(1)} %collective-permute-done.6), channel_id=1, source_target_pairs={{0,1},{1,2},{2,3},{3,4},{4,5},{5,6},{6,7},{7,8},{8,9},{9,10},{10,1... | collective-permute-start | bytes 147464 | tf_op jit(solution)/shard_map/ppermute | solution.py:39
  196.4 4.8 %collective-permute-start.14 = (bf16[16,8,192]{2,1,0:T(8,128)(2,1)S(1)}, bf16[16,8,192]{2,1,0:T(8,128)(2,1)S(1)}, u32[]{:S(2)}, u32[]{:S(2)}) collective-permute-start(bf16[16,8,192]{2,1,0:T(8,128)(2,1)S(1)} %collective-permute-done.13), channel_id=1, source_target_pairs={{0,15},{1,0},{2,1},{3,2},{4,3},{5,4},{6,5},{7,6},{8,7},{9,8},{10,9... | collective-permute-start | bytes 147464 | tf_op jit(solution)/shard_map/ppermute | solution.py:41
  209.4 4.7 %copy-start = (bf16[16,16,8,1536]{3,2,1,0:T(8,128)(2,1)}, bf16[16,16,8,1536]{3,2,1,0:T(8,128)(2,1)S(1)}, u32[]{:S(2)}) copy-start(bf16[16,16,8,1536]{3,2,1,0:T(8,128)(2,1)S(1)} %copy.20) | copy-start | bytes 18874372
  209.5 4.7 %copy-start.2 = (f32[1536]{0:T(1024)S(1)}, f32[1536]{0:T(1024)}, u32[]{:S(2)}) copy-start(f32[1536]{0:T(1024)} %param.11) | copy-start | bytes 18436
